TPU v7x, 512 devices: a whole 4x4x16 slice. The times are simulated.
512 devices in a mesh: expert: 32 (over x, y, core), replica: 16 (over z).
Axes of the slice: x: 4, y: 4, z: 16, core: 2. Of those that a mesh axis runs over, the one named last changes fastest.
Arguments:
- tokens: bfloat16 [65536, 2560], P(('expert', 'replica')), may hold values from -6 to 6
- cotangent: bfloat16 [65536, 2560], P(('expert', 'replica')), may hold values from -4 to 4
- partner: int32 [65536, 1], P(('expert', 'replica')), may hold values from 0 to 31; in each aligned block of 128 rows (0 to 127, 128 to 255, ...) at most 5 rows name the same one
- combine: int32 [65536, 2], P(('expert', 'replica')), may hold values from 1 to 8
- counts: int32 [512], P(('expert', 'replica')), may hold values from 32 to 128, as said below
- w_gate: bfloat16 [32, 2560, 768], P('expert', 'replica'), may hold values from -0.125 to 0.125
- w_up: bfloat16 [32, 2560, 768], P('expert', 'replica'), may hold values from -0.125 to 0.125
- w_down: bfloat16 [32, 768, 2560], P('expert', 'replica'), may hold values from -0.21875 to 0.21875
Outputs:
- token_grad: bfloat16 [65536, 2560], P(('expert', 'replica'))
- grad_down: bfloat16 [32, 768, 2560], P('expert', 'replica')
Inputs may be any that keep to these rules, and one draw needn't show every extreme that they name: `partner`: within the 128 rows of one device no expert index is named by more than 5 rows, and some device names one exactly 5 times. `counts`: some device has all 128 slots real.
All inputs are finite; a program needn't handle non-finite values.
Results may differ from a plain program's by a relative error of at most 0.017.
Values may be sent and summed in bfloat16 or wider, within the bound.
No kernel may reach another device: no remote copies, remote signals or barrier semaphores. Data moves between devices by JAX's collectives and lax.ppermute only.
A program may use at most 64 MiB of HBM per device.

v0:
```python
import jax
import jax.numpy as jnp
from jax import lax
from jax.sharding import PartitionSpec as P


def against_rows(left, matrix):
    return lax.dot_general(
        left, matrix, (((1,), (1,)), ((), ())), preferred_element_type=jnp.float32
    )


def expert_backward(inputs, upstream, gate_w, up_w, down_w):
    gate_act = jnp.dot(inputs, gate_w, preferred_element_type=jnp.float32)
    up_act = jnp.dot(inputs, up_w, preferred_element_type=jnp.float32)
    sigmoid_gate = jax.nn.sigmoid(gate_act)
    swish_gate = gate_act * sigmoid_gate
    hidden = (swish_gate * up_act).astype(jnp.bfloat16)
    hidden_grad = against_rows(upstream, down_w)
    gate_grad = (
        hidden_grad * up_act * sigmoid_gate * (1.0 + gate_act * (1.0 - sigmoid_gate))
    ).astype(jnp.bfloat16)
    up_grad = (hidden_grad * swish_gate).astype(jnp.bfloat16)
    input_grad = against_rows(gate_grad, gate_w) + against_rows(up_grad, up_w)
    return (hidden, input_grad)


def local(tokens, cotangent, partner, combine, counts, w_gate, w_up, w_down):
    tok_rows = tokens.shape[0]
    width = tokens.shape[1]
    expert_count = lax.axis_size("expert")
    capacity = max(2, (5 * tok_rows // 4 + expert_count - 1) // expert_count)
    positions = jnp.arange(tok_rows, dtype=jnp.int32)
    valid_rows = positions < counts[0]
    weights = combine.astype(jnp.float32)
    weight_sum = weights[:, 0] + weights[:, 1]
    share_home = jnp.where(valid_rows, weights[:, 0] / weight_sum, 0.0)
    share_away = jnp.where(valid_rows, weights[:, 1] / weight_sum, 0.0)
    upstream = cotangent.astype(jnp.float32)
    q_home = (upstream * share_home[:, None]).astype(jnp.bfloat16)
    q_away = (upstream * share_away[:, None]).astype(jnp.bfloat16)
    gate_full, up_full, down_full = (
        lax.all_gather(w_gate, "replica", axis=1, tiled=True),
        lax.all_gather(w_up, "replica", axis=1, tiled=True),
        lax.all_gather(w_down, "replica", axis=1, tiled=True),
    )
    gate_w = gate_full.reshape(gate_full.shape[1], gate_full.shape[2])
    up_w = up_full.reshape(up_full.shape[1], up_full.shape[2])
    down_w = down_full.reshape(down_full.shape[1], down_full.shape[2])
    target = partner[:, 0]
    onehot_rows = (target[:, None] == jnp.arange(expert_count, dtype=jnp.int32)[None, :]).astype(
        jnp.int32
    )
    rank_within = jnp.sum((jnp.cumsum(onehot_rows, axis=0) - onehot_rows) * onehot_rows, axis=1)
    destination = target * capacity + rank_within
    placing = (
        jnp.arange(expert_count * capacity, dtype=jnp.int32)[:, None] == destination[None, :]
    ).astype(jnp.bfloat16)
    send_x = (
        jnp.dot(placing, tokens, preferred_element_type=jnp.float32)
        .astype(jnp.bfloat16)
        .reshape(expert_count, capacity, width)
    )
    send_q = (
        jnp.dot(placing, q_away, preferred_element_type=jnp.float32)
        .astype(jnp.bfloat16)
        .reshape(expert_count, capacity, width)
    )
    hidden_home, grad_home = expert_backward(tokens, q_home, gate_w, up_w, down_w)
    x_there = lax.all_to_all(send_x, "expert", split_axis=0, concat_axis=0, tiled=True)
    q_there = lax.all_to_all(send_q, "expert", split_axis=0, concat_axis=0, tiled=True)
    item_count = x_there.shape[1]
    hidden_there, grad_there = expert_backward(
        x_there.reshape(-1, width), q_there.reshape(-1, width), gate_w, up_w, down_w
    )
    returned = lax.all_to_all(
        grad_there.astype(jnp.bfloat16).reshape(expert_count, item_count, width),
        "expert",
        split_axis=0,
        concat_axis=0,
        tiled=True,
    )
    returned, hidden_away, q_there = (
        returned,
        hidden_there.reshape(expert_count, item_count, -1),
        q_there,
    )
    contract = (((0,), (0,)), ((), ()))
    flat_returned = returned.reshape(expert_count * capacity, width)
    grad_away = lax.dot_general(
        placing, flat_returned, contract, preferred_element_type=jnp.float32
    )
    token_grad = (grad_home + grad_away).astype(jnp.bfloat16)
    flat_hidden = hidden_away.reshape(expert_count * capacity, -1)
    flat_q = q_there.reshape(expert_count * capacity, width)
    grad_down = lax.psum_scatter(
        (
            lax.dot_general(hidden_home, q_home, contract, preferred_element_type=jnp.float32)
            + lax.dot_general(flat_hidden, flat_q, contract, preferred_element_type=jnp.float32)
        ).astype(jnp.bfloat16),
        "replica",
        scatter_dimension=0,
        tiled=True,
    )
    return (token_grad, grad_down[None])


def solution(mesh):
    placed = (
        P(("expert", "replica"), None),
        P(("expert", "replica"), None),
        P(("expert", "replica"), None),
        P(("expert", "replica"), None),
        P(("expert", "replica")),
        P("expert", "replica", None),
        P("expert", "replica", None),
        P("expert", "replica", None),
    )
    return jax.shard_map(
        local,
        mesh=mesh,
        in_specs=placed,
        out_specs=(P(("expert", "replica"), None), P("expert", "replica", None)),
        check_vma=False,
    )
```

profile of v0, /device:TPU:10, one launch (start us, length us, event | category | flops | bytes accessed | tf_op | source)
XLA Modules:
  0.0 331.8 jit_solution(12413700207397267182)
XLA Ops:
  10.7 0.7 fusion.45
  11.6 0.8 select_reduce_fusion
  13.1 1.5 convolution_convert_fusion.1
  14.7 1.2 reshape.51
  15.9 9.4 %all-to-all-start = ((bf16[32,5,2560]{2,1,0:T(8,128)(2,1)}), bf16[32,5,2560]{2,1,0:T(8,128)(2,1)S(1)}, u32[]{:S(2)}, u32[]{:S(2)}) async-start(bf16[32,5,2560]{2,1,0:T(8,128)(2,1)} %reshape.51), calls=%async_computation | async-start | bytes 2621440 | tf_op jit(solution)/shard_map/all_to_all | solution.py:71
  25.7 1.3 reshape.53
  27.1 15.6 %all-to-all-done = bf16[32,5,2560]{2,1,0:T(8,128)(2,1)S(1)} async-done(((bf16[32,5,2560]{2,1,0:T(8,128)(2,1)}), bf16[32,5,2560]{2,1,0:T(8,128)(2,1)S(1)}, u32[]{:S(2)}, u32[]{:S(2)}) %all-to-all-start) | async-done | bytes 819232 | tf_op jit(solution)/shard_map/all_to_all | solution.py:71
  42.7 7.1 %all-to-all-start.1 = ((bf16[32,5,2560]{2,1,0:T(8,128)(2,1)}), bf16[32,5,2560]{2,1,0:T(8,128)(2,1)}, u32[]{:S(2)}, u32[]{:S(2)}) async-start(bf16[32,5,2560]{2,1,0:T(8,128)(2,1)} %reshape.53), calls=%async_computation.1 | async-start | bytes 2621440 | tf_op jit(solution)/shard_map/all_to_all | solution.py:70
  50.2 16.9 %all-to-all-done.1 = bf16[32,5,2560]{2,1,0:T(8,128)(2,1)} async-done(((bf16[32,5,2560]{2,1,0:T(8,128)(2,1)}), bf16[32,5,2560]{2,1,0:T(8,128)(2,1)}, u32[]{:S(2)}, u32[]{:S(2)}) %all-to-all-start.1) | async-done | bytes 819232 | tf_op jit(solution)/shard_map/all_to_all | solution.py:70
  67.1 1.5 reshape.54
  68.6 23.4 %all-gather.8.cloned.1.call-done = bf16[1,2560,768]{2,1,0:T(8,128)(2,1)} async-done(((bf16[1,160,768]{2,1,0:T(8,128)(2,1)}), bf16[1,2560,768]{2,1,0:T(8,128)(2,1)}) %all-gather.8.cloned.1.call-update) | async-done | bytes 3932176 | tf_op jit(solution)/shard_map/all_gather | solution.py:43
  92.0 2.8 fusion.6
  94.8 73.8 %all-gather.6.cloned.1.call-done = bf16[1,2560,768]{2,1,0:T(8,128)(2,1)} async-done(((bf16[1,160,768]{2,1,0:T(8,128)(2,1)}), bf16[1,2560,768]{2,1,0:T(8,128)(2,1)}) %all-gather.6.cloned.1.call-update) | async-done | bytes 3932176 | tf_op jit(solution)/shard_map/all_gather | solution.py:44
  168.6 2.9 fusion.14
  171.6 3.1 fusion.2
  174.6 0.8 fusion.10
  175.7 1.3 fusion.36
  177.0 3.2 add_convert_fusion
  180.2 64.9 %all-gather.4.cloned.1.call-done = bf16[1,768,2560]{2,1,0:T(8,128)(2,1)} async-done(((bf16[1,48,2560]{2,1,0:T(8,128)(2,1)}), bf16[1,768,2560]{2,1,0:T(8,128)(2,1)}) %all-gather.4.cloned.1.call-update) | async-done | bytes 3932176 | tf_op jit(solution)/shard_map/all_gather | solution.py:45
  245.1 3.7 %fusion.16 = f32[160,768]{1,0:T(8,128)S(1)} fusion(bf16[160,2560]{1,0:T(8,128)(2,1)S(1)} %reshape.52, bf16[1,768,2560]{2,1,0:T(8,128)(2,1)} %all-gather.4.cloned.1.call-done), kind=kOutput, calls=%fused_computation.17 | convolution fusion | flops 629145600 | bytes 5242880 | tf_op jit(solution)/shard_map/dot_general | solution.py:8
  248.9 1.4 fusion
  251.0 1.4 fusion.26
  252.4 1.3 reshape.55
  253.7 7.6 %all-to-all-start.2 = ((bf16[32,5,2560]{2,1,0:T(8,128)(2,1)}), bf16[32,5,2560]{2,1,0:T(8,128)(2,1)}, u32[]{:S(2)}, u32[]{:S(2)}) async-start(bf16[32,5,2560]{2,1,0:T(8,128)(2,1)} %reshape.55), calls=%async_computation.2 | async-start | bytes 2621440 | tf_op jit(solution)/shard_map/all_to_all | solution.py:76
  261.3 3.7 %fusion.18 = f32[128,768]{1,0:T(8,128)S(1)} fusion(bf16[1,768,2560]{2,1,0:T(8,128)(2,1)} %all-gather.4.cloned.1.call-done, bf16[128,2560]{1,0:T(8,128)(2,1)S(1)} %copy-done.7, f32[128]{0:T(128)S(1)} %get-tuple-element.3), kind=kOutput, calls=%fused_computation.19 | convolution fusion | flops 504299520 | bytes 4981248 | tf_op jit(solution)/shard_map/dot_general | solution.py:8
  265.0 1.4 fusion.4
  266.4 0.7 copy-done.3
  267.1 1.4 fusion.23
  268.5 10.0 %all-to-all-done.2 = bf16[32,5,2560]{2,1,0:T(8,128)(2,1)} async-done(((bf16[32,5,2560]{2,1,0:T(8,128)(2,1)}), bf16[32,5,2560]{2,1,0:T(8,128)(2,1)}, u32[]{:S(2)}, u32[]{:S(2)}) %all-to-all-start.2) | async-done | bytes 819232 | tf_op jit(solution)/shard_map/all_to_all | solution.py:76
  278.5 1.5 reshape.56
  280.0 1.2 fusion.29
  281.2 44.0 %reduce-scatter.2.cloned.1.call-done = bf16[48,2560]{1,0:T(8,128)(2,1)} async-done(((bf16[768,2560]{1,0:T(8,128)(2,1)}), bf16[48,2560]{1,0:T(8,128)(2,1)}) %reduce-scatter.2.cloned.1.call-update) | async-done | bytes 245776 | tf_op jit(solution)/shard_map/reduce_scatter | solution.py:96
  (37 shorter events, 5.5 us)
Async XLA Ops:
  7.2 18.2 %copy-start = (bf16[128,2560]{1,0:T(8,128)(2,1)S(1)}, bf16[128,2560]{1,0:T(8,128)(2,1)}, u32[]{:S(2)}) copy-start(bf16[128,2560]{1,0:T(8,128)(2,1)} %param.8) | copy-start | bytes 1966084
  7.2 84.8 %all-gather.8.cloned.1.call-start = ((), (), s32[]{:S(2)}) async-start(), calls=%async_computation.6 | async-start | bytes 4177920 | tf_op jit(solution)/shard_map/all_gather | solution.py:43
  7.9 160.7 %all-gather.6.cloned.1.call-start = ((), (), s32[]{:S(2)}) async-start(), calls=%async_computation.5 | async-start | bytes 4177920 | tf_op jit(solution)/shard_map/all_gather | solution.py:44
  8.7 236.5 %all-gather.4.cloned.1.call-start = ((), (), s32[]{:S(2)}) async-start(), calls=%async_computation.4 | async-start | bytes 4177920 | tf_op jit(solution)/shard_map/all_gather | solution.py:45
  15.9 26.7 %all-to-all-start = ((bf16[32,5,2560]{2,1,0:T(8,128)(2,1)}), bf16[32,5,2560]{2,1,0:T(8,128)(2,1)S(1)}, u32[]{:S(2)}, u32[]{:S(2)}) async-start(bf16[32,5,2560]{2,1,0:T(8,128)(2,1)} %reshape.51), calls=%async_computation | async-start | bytes 2621440 | tf_op jit(solution)/shard_map/all_to_all | solution.py:71
  42.7 24.4 %all-to-all-start.1 = ((bf16[32,5,2560]{2,1,0:T(8,128)(2,1)}), bf16[32,5,2560]{2,1,0:T(8,128)(2,1)}, u32[]{:S(2)}, u32[]{:S(2)}) async-start(bf16[32,5,2560]{2,1,0:T(8,128)(2,1)} %reshape.53), calls=%async_computation.1 | async-start | bytes 2621440 | tf_op jit(solution)/shard_map/all_to_all | solution.py:70
  49.8 275.5 %reduce-scatter.2.cloned.1.call-start = ((), (), s32[]{:S(2)}) async-start(), calls=%async_computation.7 | async-start | bytes 4177920 | tf_op jit(solution)/shard_map/reduce_scatter | solution.py:96
  168.6 6.0 %copy-start.1 = (bf16[1,2560,768]{2,1,0:T(8,128)(2,1)S(1)}, bf16[1,2560,768]{2,1,0:T(8,128)(2,1)}, u32[]{:S(2)}) copy-start(bf16[1,2560,768]{2,1,0:T(8,128)(2,1)} %all-gather.6.cloned.1.call-done) | copy-start | bytes 11796484
  171.5 3.9 %copy-start.10 = (f32[128,768]{1,0:T(8,128)}, f32[128,768]{1,0:T(8,128)S(1)}, u32[]{:S(2)}) copy-start(f32[128,768]{1,0:T(8,128)S(1)} %fusion.14) | copy-start | bytes 1179652
  174.6 1.1 copy-start.6
  175.4 1.6 copy-start.8
  180.2 68.6 %copy-start.9 = (f32[160,768]{1,0:T(8,128)S(1)}, f32[160,768]{1,0:T(8,128)}, u32[]{:S(2)}) copy-start(f32[160,768]{1,0:T(8,128)} %copy-done.8) | copy-start | bytes 1474564
  245.1 3.7 %copy-start.4 = (bf16[1,2560,768]{2,1,0:T(8,128)(2,1)S(1)}, bf16[1,2560,768]{2,1,0:T(8,128)(2,1)}, u32[]{:S(2)}) copy-start(bf16[1,2560,768]{2,1,0:T(8,128)(2,1)} %all-gather.8.cloned.1.call-done) | copy-start | bytes 11796484
  248.9 2.1 copy-start.2
  252.4 8.9 %copy-start.7 = (bf16[128,2560]{1,0:T(8,128)(2,1)S(1)}, bf16[128,2560]{1,0:T(8,128)(2,1)}, u32[]{:S(2)}) copy-start(bf16[128,2560]{1,0:T(8,128)(2,1)} %param.9) | copy-start | bytes 1966084
  253.7 11.3 %copy-start.11 = (f32[128,768]{1,0:T(8,128)S(1)}, f32[128,768]{1,0:T(8,128)}, u32[]{:S(2)}) copy-start(f32[128,768]{1,0:T(8,128)} %copy-done.10) | copy-start | bytes 1179652
  253.7 24.9 %all-to-all-start.2 = ((bf16[32,5,2560]{2,1,0:T(8,128)(2,1)}), bf16[32,5,2560]{2,1,0:T(8,128)(2,1)}, u32[]{:S(2)}, u32[]{:S(2)}) async-start(bf16[32,5,2560]{2,1,0:T(8,128)(2,1)} %reshape.55), calls=%async_computation.2 | async-start | bytes 2621440 | tf_op jit(solution)/shard_map/all_to_all | solution.py:76
  261.3 3.7 %copy-start.5 = (bf16[1,2560,768]{2,1,0:T(8,128)(2,1)S(1)}, bf16[1,2560,768]{2,1,0:T(8,128)(2,1)}, u32[]{:S(2)}) copy-start(bf16[1,2560,768]{2,1,0:T(8,128)(2,1)} %all-gather.8.cloned.1.call-done) | copy-start | bytes 11796484
  265.0 2.1 copy-start.3
Sparse Core Ops, SparseCore 0:
  10.1 81.8 all-gather.7
  94.1 74.4 all-gather.5
  170.7 74.4 all-gather.3
  248.4 76.7 reduce-scatter.1
where the time goes:
time: 333 us; the launch traced here: 332 us
  waiting for transfers between devices  251 us (75%)
  matrix products  30.2 us (9%)
  starting transfers between devices  24.2 us (7%)
  between operations  14.7 us (4%)
  local copies, waits for them, and re-layouts  8.84 us (3%)
    all_gather x1, waiting for transfers between devices, local(): lax.all_gather(w_up, 'replica', axis=1, tiled=True)  73.8 us
    all_gather x1, waiting for transfers between devices, local(): lax.all_gather(w_down, 'replica', axis=1, tiled=True)  64.9 us
    reduce_scatter x1, waiting for transfers between devices, local(): lax.psum_scatter((lax.dot_general(hidden_home, q_home, contract, preferre...  44 us
    all_gather x1, waiting for transfers between devices, local(): lax.all_gather(w_gate, 'replica', axis=1, tiled=True)  23.4 us
    all_to_all x1, waiting for transfers between devices, local(): lax.all_to_all(send_x, 'expert', split_axis=0, concat_axis=0, tiled=True)  16.9 us
    all_to_all x1, waiting for transfers between devices, local(): lax.all_to_all(send_q, 'expert', split_axis=0, concat_axis=0, tiled=True)  15.6 us
    dot_general x6, matrix products, against_rows(): lax.dot_general(left, matrix, (((1,), (1,)), ((), ())), preferred_element...  13 us
    all_to_all x1, waiting for transfers between devices, local(): lax.all_to_all(grad_there.astype(jnp.bfloat16).reshape(expert_count, item...  9.99 us
  transfers between devices with their start and end apart: 7, of which 7 were waited for; matrix products, arithmetic and copies ran while one was open for 12% of the time, Pallas kernels for 0%

commit v1 on v0

--- a/solution.py
+++ b/solution.py
@@ -41,7 +41,9 @@
     q_away = (upstream * share_away[:, None]).astype(jnp.bfloat16)
     gate_full, up_full, down_full = (
         lax.all_gather(w_gate, "replica", axis=1, tiled=True),
-        lax.all_gather(w_up, "replica", axis=1, tiled=True),
+        jnp.concatenate(
+            lax.all_to_all(jnp.stack([w_up] * lax.axis_size("replica")), "replica", 0, 0), axis=1
+        ),
         lax.all_gather(w_down, "replica", axis=1, tiled=True),
     )
     gate_w = gate_full.reshape(gate_full.shape[1], gate_full.shape[2])

time: 333 us -> 461 us (1.38)
  the two profiles are of different devices: /device:TPU:10 before, /device:TPU:2 now
where the time goes in v1:
time: 461 us; the launch traced here: 460 us
  waiting for transfers between devices  340 us (74%)
  matrix products  35.8 us (8%)
  starting transfers between devices  30.6 us (7%)
  blocking collectives  26.1 us (6%)
  between operations  14.7 us (3%)
  local copies, waits for them, and re-layouts  9.78 us (2%)
    all_gather x1, waiting for transfers between devices, local(): lax.all_gather(w_gate, 'replica', axis=1, tiled=True)  213 us
    all_gather x1, waiting for transfers between devices, local(): lax.all_gather(w_down, 'replica', axis=1, tiled=True)  59.4 us
    reduce_scatter x1, waiting for transfers between devices, local(): lax.psum_scatter((lax.dot_general(hidden_home, q_home, contract, preferre...  39.4 us
    all_to_all x1, blocking collectives, local(): lax.all_to_all(send_x, 'expert', split_axis=0, concat_axis=0, tiled=True)  26.1 us
    dot_general x6, matrix products, against_rows(): lax.dot_general(left, matrix, (((1,), (1,)), ((), ())), preferred_element...  17.2 us
    all_to_all x1, waiting for transfers between devices, local(): lax.all_to_all(send_q, 'expert', split_axis=0, concat_axis=0, tiled=True)  15.6 us
    all_to_all x1, starting transfers between devices, local(): lax.all_to_all(jnp.stack([w_up] * lax.axis_size('replica')), 'replica', 0...  13.3 us
    all_to_all x1, waiting for transfers between devices, local(): lax.all_to_all(grad_there.astype(jnp.bfloat16).reshape(expert_count, item...  11 us
  transfers between devices with their start and end apart: 6, of which 5 were waited for; matrix products, arithmetic and copies ran while one was open for 9% of the time, Pallas kernels for 0%

profile of v1, /device:TPU:2, one launch (start us, length us, event | category | flops | bytes accessed | tf_op | source)
XLA Modules:
  0.0 460.0 jit_solution(14648983725689794678)
XLA Ops:
  7.9 0.7 convert_element_type.50
  8.6 0.7 fusion.39
  9.5 0.8 select_reduce_fusion
  11.0 1.5 convolution_convert_fusion.1
  12.5 1.2 reshape.50
  13.8 9.7 %all-to-all-start.1 = ((bf16[32,5,2560]{2,1,0:T(8,128)(2,1)}), bf16[32,5,2560]{2,1,0:T(8,128)(2,1)S(1)}, u32[]{:S(2)}, u32[]{:S(2)}) async-start(bf16[32,5,2560]{2,1,0:T(8,128)(2,1)} %reshape.50), calls=%async_computation.1 | async-start | bytes 2621440 | tf_op jit(solution)/shard_map/all_to_all | solution.py:73
  23.8 1.3 reshape.52
  25.1 15.6 %all-to-all-done.1 = bf16[32,5,2560]{2,1,0:T(8,128)(2,1)S(1)} async-done(((bf16[32,5,2560]{2,1,0:T(8,128)(2,1)}), bf16[32,5,2560]{2,1,0:T(8,128)(2,1)S(1)}, u32[]{:S(2)}, u32[]{:S(2)}) %all-to-all-start.1) | async-done | bytes 819232 | tf_op jit(solution)/shard_map/all_to_all | solution.py:73
  40.7 26.1 %all_to_all.20 = bf16[32,5,2560]{2,1,0:T(8,128)(2,1)} all-to-all(bf16[32,5,2560]{2,1,0:T(8,128)(2,1)} %reshape.52), channel_id=1, replica_groups=mesh['expert'=32,'replica'=16] {'expert'}, dimensions={0} | all-to-all | bytes 1638400 | tf_op jit(solution)/shard_map/all_to_all | solution.py:72
  66.9 2.3 stack.2
  69.2 13.3 %all-to-all-start = ((bf16[16,1,160,768]{3,2,1,0:T(8,128)(2,1)}), bf16[16,1,160,768]{3,2,1,0:T(8,128)(2,1)}, u32[]{:S(2)}, u32[]{:S(2)}) async-start(bf16[16,1,160,768]{3,2,1,0:T(8,128)(2,1)} %stack.2), calls=%async_computation | async-start | bytes 7864320 | tf_op jit(solution)/shard_map/all_to_all | solution.py:45
  83.3 0.7 all-gather.3.cloned.1.call-update
  84.4 1.5 reshape.53
  85.9 213.0 %all-gather.5.cloned.1.call-done = bf16[1,2560,768]{2,1,0:T(8,128)(2,1)} async-done(((bf16[1,160,768]{2,1,0:T(8,128)(2,1)}), bf16[1,2560,768]{2,1,0:T(8,128)(2,1)}) %all-gather.5.cloned.1.call-update) | async-done | bytes 3932176 | tf_op jit(solution)/shard_map/all_gather | solution.py:43
  298.9 2.9 fusion.6
  302.2 0.8 fusion.2
  303.0 2.9 fusion.51
  305.9 3.1 fusion.52
  309.0 1.3 fusion.28
  310.3 3.2 add_convert_fusion
  313.5 59.4 %all-gather.3.cloned.1.call-done = bf16[1,768,2560]{2,1,0:T(8,128)(2,1)} async-done(((bf16[1,48,2560]{2,1,0:T(8,128)(2,1)}), bf16[1,768,2560]{2,1,0:T(8,128)(2,1)}) %all-gather.3.cloned.1.call-update) | async-done | bytes 3932176 | tf_op jit(solution)/shard_map/all_gather | solution.py:47
  372.9 3.7 fusion.10
  376.6 1.4 fusion.8
  378.0 3.7 fusion.31
  381.7 2.3 fusion.18
  384.0 2.3 reshape.54
  386.3 7.6 %all-to-all-start.3 = ((bf16[32,5,2560]{2,1,0:T(8,128)(2,1)}), bf16[32,5,2560]{2,1,0:T(8,128)(2,1)S(1)}, u32[]{:S(2)}, u32[]{:S(2)}) async-start(bf16[32,5,2560]{2,1,0:T(8,128)(2,1)} %reshape.54), calls=%async_computation.3 | async-start | bytes 2621440 | tf_op jit(solution)/shard_map/all_to_all | solution.py:78
  393.9 3.6 fusion.33
  397.6 2.5 fusion.15
  400.1 11.0 %all-to-all-done.3 = bf16[32,5,2560]{2,1,0:T(8,128)(2,1)S(1)} async-done(((bf16[32,5,2560]{2,1,0:T(8,128)(2,1)}), bf16[32,5,2560]{2,1,0:T(8,128)(2,1)S(1)}, u32[]{:S(2)}, u32[]{:S(2)}) %all-to-all-start.3) | async-done | bytes 819232 | tf_op jit(solution)/shard_map/all_to_all | solution.py:78
  411.5 2.5 fusion.21
  414.0 39.4 %reduce-scatter.2.cloned.1.call-done = bf16[48,2560]{1,0:T(8,128)(2,1)} async-done(((bf16[768,2560]{1,0:T(8,128)(2,1)}), bf16[48,2560]{1,0:T(8,128)(2,1)}) %reduce-scatter.2.cloned.1.call-update) | async-done | bytes 245776 | tf_op jit(solution)/shard_map/reduce_scatter | solution.py:98
  (36 shorter events, 3.2 us)
Async XLA Ops:
  7.2 16.3 %copy-start = (bf16[128,2560]{1,0:T(8,128)(2,1)S(1)}, bf16[128,2560]{1,0:T(8,128)(2,1)}, u32[]{:S(2)}) copy-start(bf16[128,2560]{1,0:T(8,128)(2,1)} %param.8) | copy-start | bytes 1966084
  13.8 53.1 %copy-start.11 = (bf16[1,160,768]{2,1,0:T(8,128)(2,1)S(1)}, bf16[1,160,768]{2,1,0:T(8,128)(2,1)}, u32[]{:S(2)}) copy-start(bf16[1,160,768]{2,1,0:T(8,128)(2,1)} %param.14) | copy-start | bytes 737284
  13.8 27.0 %all-to-all-start.1 = ((bf16[32,5,2560]{2,1,0:T(8,128)(2,1)}), bf16[32,5,2560]{2,1,0:T(8,128)(2,1)S(1)}, u32[]{:S(2)}, u32[]{:S(2)}) async-start(bf16[32,5,2560]{2,1,0:T(8,128)(2,1)} %reshape.50), calls=%async_computation.1 | async-start | bytes 2621440 | tf_op jit(solution)/shard_map/all_to_all | solution.py:73
  69.2 233.8 %all-to-all-start = ((bf16[16,1,160,768]{3,2,1,0:T(8,128)(2,1)}), bf16[16,1,160,768]{3,2,1,0:T(8,128)(2,1)}, u32[]{:S(2)}, u32[]{:S(2)}) async-start(bf16[16,1,160,768]{3,2,1,0:T(8,128)(2,1)} %stack.2), calls=%async_computation | async-start | bytes 7864320 | tf_op jit(solution)/shard_map/all_to_all | solution.py:45
  82.5 216.4 %all-gather.5.cloned.1.call-start = ((), (), s32[]{:S(2)}) async-start(), calls=%async_computation.6 | async-start | bytes 4177920 | tf_op jit(solution)/shard_map/all_gather | solution.py:43
  83.2 289.6 %all-gather.3.cloned.1.call-start = ((), (), s32[]{:S(2)}) async-start(), calls=%async_computation.5 | async-start | bytes 4177920 | tf_op jit(solution)/shard_map/all_gather | solution.py:47
  84.0 369.4 %reduce-scatter.2.cloned.1.call-start = ((), (), s32[]{:S(2)}) async-start(), calls=%async_computation.7 | async-start | bytes 4177920 | tf_op jit(solution)/shard_map/reduce_scatter | solution.py:98
  298.9 3.3 copy-start.1
  303.0 6.0 %copy-start.5 = (bf16[128,2560]{1,0:T(8,128)(2,1)S(1)}, bf16[128,2560]{1,0:T(8,128)(2,1)}, u32[]{:S(2)}) copy-start(bf16[128,2560]{1,0:T(8,128)(2,1)} %param.9) | copy-start | bytes 1966084
  305.9 3.1 copy-start.9
  308.9 1.3 copy-start.7
  313.5 59.4 %copy-start.6 = (bf16[128,2560]{1,0:T(8,128)(2,1)S(1)}, bf16[128,2560]{1,0:T(8,128)(2,1)}, u32[]{:S(2)}) copy-start(bf16[128,2560]{1,0:T(8,128)(2,1)} %param.9) | copy-start | bytes 1966084
  372.9 3.7 copy-start.4
  378.0 3.7 copy-start.2
  378.0 3.7 copy-start.8
  386.3 11.3 %copy-start.10 = (f32[128,768]{1,0:T(8,128)S(1)}, f32[128,768]{1,0:T(8,128)}, u32[]{:S(2)}) copy-start(f32[128,768]{1,0:T(8,128)} %copy-done.9) | copy-start | bytes 1179652
  386.3 24.8 %all-to-all-start.3 = ((bf16[32,5,2560]{2,1,0:T(8,128)(2,1)}), bf16[32,5,2560]{2,1,0:T(8,128)(2,1)S(1)}, u32[]{:S(2)}, u32[]{:S(2)}) async-start(bf16[32,5,2560]{2,1,0:T(8,128)(2,1)} %reshape.54), calls=%async_computation.3 | async-start | bytes 2621440 | tf_op jit(solution)/shard_map/all_to_all | solution.py:78
  393.9 3.7 copy-start.3
Sparse Core Ops, SparseCore 0:
  85.4 213.4 all-gather.4
  301.0 71.8 all-gather.2
  376.3 77.0 reduce-scatter.1
